TPU v7x, 128 devices: a whole 4x4x4 slice. The times are simulated.
128 devices in a mesh: dp: 4 (over z_hi, core), mp: 32 (over x, y, z_lo).
Axes of the slice: x: 4, y: 4, z: 4 (z_hi: 2, z_lo: 2; z = z_hi * 2 + z_lo), core: 2. Of those that a mesh axis runs over, the one named last changes fastest.
Arguments:
- residual_input: bfloat16 [2048, 4608], P(('dp', 'mp')), may hold values from -6 to 6
- before_attention_gain: float32 [4608], replicated, may hold values from 0.25 to 1.75
- after_attention_gain: float32 [4608], replicated, may hold values from 0.25 to 1.75
- before_feedforward_gain: float32 [4608], replicated, may hold values from 0.25 to 1.75
- after_feedforward_gain: float32 [4608], replicated, may hold values from 0.25 to 1.75
- query_weight: bfloat16 [4608, 4096], P(None, 'mp'), may hold values from -0.09375 to 0.09375
- key_value_weight: bfloat16 [4608, 2, 32, 128], P(None, None, 'mp'), as said below
- output_weight: bfloat16 [4096, 4608], P('mp'), may hold values from -0.09375 to 0.09375
- gate_matrix: bfloat16 [4608, 20480], P(None, 'mp'), may hold values from -0.09375 to 0.09375
- up_matrix: bfloat16 [4608, 20480], P(None, 'mp'), may hold values from -0.09375 to 0.09375
- down_matrix: bfloat16 [20480, 4608], P('mp'), may hold values from -0.0390625 to 0.0390625
- key_value_cache: bfloat16 [256, 2, 32, 16, 128], P('dp', None, 'mp'), as said below
- projected_lowrank_left: bfloat16 [64, 4608, 16], P('mp'), may hold values from -0.09375 to 0.09375
- projected_lowrank_right: bfloat16 [64, 16, 3, 32, 128], P(None, None, None, 'mp'), as said below
- result_lowrank_left: bfloat16 [64, 4096, 16], P(None, 'mp'), may hold values from -0.09375 to 0.09375
- result_lowrank_right: bfloat16 [64, 16, 4608], P('mp'), may hold values from -1.5 to 1.5
- token_request: int32 [4, 512], P('dp'), may hold values from 0 to 7, never falling along the last dimension, each value on 1 to 256 neighbouring positions
- lowrank_choice_by_prompt: int32 [4, 8], P('dp'), may hold values from 0 to 63
- adapter_position: int32 [64], replicated, may hold values from 0 to 63, each once
- request_pages: int32 [4, 8, 4], replicated, may hold values from 0 to 255
Outputs:
- hidden_out: bfloat16 [2048, 4608], P(('dp', 'mp'))
- kv_new: bfloat16 [2048, 2, 32, 128], P('dp', None, 'mp')
Inputs may be any that keep to these rules, and one draw needn't show every extreme that they name: `key_value_weight`: query heads h and h2 with h // 2 == h2 // 2 have equal key and value weights: they share one key and value head. `key_value_cache`: query heads that share a key and value head have equal cached keys and values. `projected_lowrank_right`: the key and value parts of query heads that share a key and value head are equal. `token_request`: numbers never fall along a group; every request has at least one token. `adapter_position`: each slot once. `request_pages`: pages may repeat within and across requests.
All inputs are finite; a program needn't handle non-finite values.
Results may differ from a plain program's by a relative error of at most 0.035.
Values may be sent and summed in bfloat16 or wider, within the bound.
No kernel may reach another device: no remote copies, remote signals or barrier semaphores. Data moves between devices by JAX's collectives and lax.ppermute only.
A program may use at most 128 MiB of HBM per device.

v0:
```python
import math
import jax
import jax.numpy as jnp
from jax import lax
from jax.sharding import PartitionSpec as P

HIDDEN_BREADTH = 4608
ASKING_CHANNELS = 32
CHANNEL_LENGTH = 128
NUM_LOW_TERMS = 64
LOW_DIMENSION = 16
SHARD_PROMPTS = 8
PPR = 4
PAGE = 16
EPS = 1e-06
SOFTCAP = 50.0
DP_AXES = ("zh", "c")
MP_AXES = ("x", "y", "zl")
MP_STAGES = (("zl",), ("x", "y"))


def gather_mp(values):
    for stage in MP_STAGES:
        values = lax.all_gather(values, stage, axis=0, tiled=True)
    return values


def scatter_mp(values):
    for stage in reversed(MP_STAGES):
        values = lax.psum_scatter(values, stage, scatter_dimension=0, tiled=True)
    return values


def sum_mp(values):
    for stage in MP_STAGES:
        values = lax.psum(values, stage)
    return values


def rms_scale(values, scaling):
    mean_square = jnp.mean(values * values, axis=-1, keepdims=True)
    return values * lax.rsqrt(mean_square + EPS) * scaling


def apply_rotary(values, token_positions):
    half_dim = values.shape[-1] // 2
    frequency = 10000.0 ** (-2.0 * jnp.arange(half_dim, dtype=jnp.float32) / values.shape[-1])
    angles = token_positions.astype(jnp.float32)[:, None] * frequency[None, :]
    cosine = jnp.cos(angles)[:, None, :]
    sine_part = jnp.sin(angles)[:, None, :]
    first_half = values[..., :half_dim]
    second_half = values[..., half_dim:]
    return jnp.concatenate(
        [
            first_half * cosine - second_half * sine_part,
            second_half * cosine + first_half * sine_part,
        ],
        axis=-1,
    )


def positions_of(segments):
    length = segments.shape[0]
    earlier = jnp.sum((segments[None, :] < segments[:, None]).astype(jnp.int32), axis=1)
    return PPR * PAGE + jnp.arange(length, dtype=jnp.int32) - earlier


def capped(scores):
    return SOFTCAP * jnp.tanh(scores / SOFTCAP)


def attend_local(query_rows, keys_new, fresh_values, keys_pre, values_pre, segments):
    scale_factor = 1.0 / math.sqrt(HIDDEN_BREADTH // ASKING_CHANNELS)
    length = segments.shape[0]
    prefix_owner = jnp.arange(keys_pre.shape[1], dtype=jnp.int32) // (PPR * PAGE)
    mask_pre = (prefix_owner[None, :] == segments[:, None])[None]
    ordinal = jnp.arange(length, dtype=jnp.int32)
    mask_new = ((segments[None, :] == segments[:, None]) & (ordinal[None, :] <= ordinal[:, None]))[
        None
    ]
    scores_pre = (
        jnp.einsum("thd,hjd->htj", query_rows, keys_pre, preferred_element_type=jnp.float32)
        * scale_factor
    )
    scores_new = (
        jnp.einsum("thd,uhd->htu", query_rows, keys_new, preferred_element_type=jnp.float32)
        * scale_factor
    )
    weight_pre = jnp.where(mask_pre, jnp.exp(capped(scores_pre)), 0.0)
    weight_new = jnp.where(mask_new, jnp.exp(capped(scores_new)), 0.0)
    totals = jnp.sum(weight_pre, axis=-1, keepdims=True) + jnp.sum(
        weight_new, axis=-1, keepdims=True
    )
    probs_pre = (weight_pre / totals).astype(jnp.bfloat16)
    probs_new = (weight_new / totals).astype(jnp.bfloat16)
    mixture = jnp.einsum("htj,hjd->thd", probs_pre, values_pre, preferred_element_type=jnp.float32)
    mixture = mixture + jnp.einsum(
        "htu,uhd->thd", probs_new, fresh_values, preferred_element_type=jnp.float32
    )
    return mixture.astype(jnp.bfloat16).reshape(length, -1)


def shards(
    residual_input,
    before_attention_gain,
    after_attention_gain,
    before_feedforward_gain,
    after_feedforward_gain,
    query_weight,
    key_value_weight,
    output_weight,
    gate_matrix,
    up_matrix,
    down_matrix,
    key_value_cache,
    projected_lowrank_left,
    projected_lowrank_right,
    result_lowrank_left,
    result_lowrank_right,
    token_request,
    lowrank_choice_by_prompt,
    adapter_position,
    request_pages,
):
    mp_index = lax.axis_index(MP_AXES)
    dp_index = lax.axis_index(DP_AXES)
    residual = residual_input.astype(jnp.float32)
    normed_rows = rms_scale(residual, before_attention_gain).astype(jnp.bfloat16)
    normalized_rows = gather_mp(normed_rows)
    prompt_ordinal = normalized_rows.shape[0]
    channel_window = query_weight.shape[1] // CHANNEL_LENGTH
    query_rows = jnp.dot(normalized_rows, query_weight, preferred_element_type=jnp.float32).reshape(
        prompt_ordinal, channel_window, CHANNEL_LENGTH
    )
    key_value_rows = jnp.dot(
        normalized_rows,
        key_value_weight.reshape(HIDDEN_BREADTH, 2 * channel_window * CHANNEL_LENGTH),
        preferred_element_type=jnp.float32,
    ).reshape(prompt_ordinal, 2, channel_window, CHANNEL_LENGTH)
    segments = token_request[0]
    request_ids = lowrank_choice_by_prompt[0]
    request_range = jnp.arange(SHARD_PROMPTS, dtype=jnp.int32)
    membership = segments[:, None] == request_range[None, :]
    adapter_range = jnp.arange(NUM_LOW_TERMS, dtype=jnp.int32)
    token_adapter = jnp.sum(jnp.where(membership, request_ids[None, :], 0), axis=1)
    token_adapter_slot = jnp.sum(
        jnp.where(token_adapter[:, None] == adapter_range[None, :], adapter_position[None, :], 0),
        axis=1,
    )
    seat_count = projected_lowrank_left.shape[0]
    local_seats = mp_index * seat_count + jnp.arange(seat_count, dtype=jnp.int32)
    seat_factors = jnp.einsum(
        "td,sdk->tsk", normalized_rows, projected_lowrank_left, preferred_element_type=jnp.float32
    )
    seat_here = token_adapter_slot[:, None] == local_seats[None, :]
    lowrank_source = jnp.sum(jnp.where(seat_here[:, :, None], seat_factors, 0.0), axis=1)
    lowrank_source = sum_mp(lowrank_source.astype(jnp.bfloat16))
    choice_mask_table = membership.astype(jnp.bfloat16)
    broadened_lines = (choice_mask_table[:, :, None] * lowrank_source[:, None, :]).reshape(
        prompt_ordinal, SHARD_PROMPTS * LOW_DIMENSION
    )
    raised_result_lines = projected_lowrank_right[request_ids].reshape(
        SHARD_PROMPTS * LOW_DIMENSION, 3 * channel_window * CHANNEL_LENGTH
    )
    adapter_query_key_value = jnp.dot(
        broadened_lines, raised_result_lines, preferred_element_type=jnp.float32
    ).reshape(prompt_ordinal, 3, channel_window, CHANNEL_LENGTH)
    token_positions = positions_of(segments)
    rotary_queries = apply_rotary(
        query_rows + adapter_query_key_value[:, 0], token_positions
    ).astype(jnp.bfloat16)
    rotary_keys = apply_rotary(
        key_value_rows[:, 0] + adapter_query_key_value[:, 1], token_positions
    ).astype(jnp.bfloat16)
    fresh_values = (key_value_rows[:, 1] + adapter_query_key_value[:, 2]).astype(jnp.bfloat16)
    kv_new = jnp.stack([rotary_keys, fresh_values], axis=1)
    own_pages = lax.dynamic_index_in_dim(request_pages, dp_index, 0, keepdims=False).reshape(
        SHARD_PROMPTS * PPR
    )
    whole_pool = lax.all_gather(key_value_cache, DP_AXES, axis=0, tiled=True)
    chosen = whole_pool[own_pages]
    keys_pre = jnp.transpose(chosen[:, 0], (1, 0, 2, 3)).reshape(
        channel_window, SHARD_PROMPTS * PPR * PAGE, CHANNEL_LENGTH
    )
    values_pre = jnp.transpose(chosen[:, 1], (1, 0, 2, 3)).reshape(
        channel_window, SHARD_PROMPTS * PPR * PAGE, CHANNEL_LENGTH
    )
    attended = attend_local(
        rotary_queries, rotary_keys, fresh_values, keys_pre, values_pre, segments
    )
    request_output_down = result_lowrank_left[request_ids]
    request_output_factors = jnp.einsum(
        "tc,rck->trk", attended, request_output_down, preferred_element_type=jnp.float32
    )
    output_adapter_piece = jnp.sum(
        jnp.where(membership[:, :, None], request_output_factors, 0.0), axis=1
    )
    result_lowrank_source = sum_mp(output_adapter_piece).astype(jnp.bfloat16)
    result_seat_lines = result_lowrank_right.shape[0]
    output_slots = mp_index * result_seat_lines + jnp.arange(result_seat_lines, dtype=jnp.int32)
    resident_here = (token_adapter_slot[:, None] == output_slots[None, :]).astype(jnp.bfloat16)
    broadened_result = (resident_here[:, :, None] * result_lowrank_source[:, None, :]).reshape(
        prompt_ordinal, result_seat_lines * LOW_DIMENSION
    )
    raised_window = result_lowrank_right.reshape(result_seat_lines * LOW_DIMENSION, HIDDEN_BREADTH)
    attn_sum = scatter_mp(
        (
            jnp.dot(attended, output_weight, preferred_element_type=jnp.float32)
            + jnp.dot(broadened_result, raised_window, preferred_element_type=jnp.float32)
        ).astype(jnp.bfloat16)
    ).astype(jnp.float32)
    after_attn = (residual + rms_scale(attn_sum, after_attention_gain)).astype(jnp.bfloat16)
    normed_ffw = rms_scale(after_attn.astype(jnp.float32), before_feedforward_gain).astype(
        jnp.bfloat16
    )
    piece = gather_mp(normed_ffw)
    gated = jnp.dot(piece, gate_matrix, preferred_element_type=jnp.float32)
    upward = jnp.dot(piece, up_matrix, preferred_element_type=jnp.float32)
    hidden = (jax.nn.gelu(gated, approximate=True) * upward).astype(jnp.bfloat16)
    ffw_sum = scatter_mp(
        jnp.dot(hidden, down_matrix, preferred_element_type=jnp.float32).astype(jnp.bfloat16)
    ).astype(jnp.float32)
    hidden_out = (
        after_attn.astype(jnp.float32) + rms_scale(ffw_sum, after_feedforward_gain)
    ).astype(jnp.bfloat16)
    return (hidden_out, kv_new)


def solution(mesh):
    fine_mesh = jax.sharding.Mesh(mesh.devices.reshape(2, 2, 4, 4, 2), DP_AXES + MP_AXES)
    return jax.shard_map(
        shards,
        mesh=fine_mesh,
        in_specs=(
            P(DP_AXES + MP_AXES, None),
            P(),
            P(),
            P(),
            P(),
            P(None, MP_AXES),
            P(None, None, MP_AXES, None),
            P(MP_AXES, None),
            P(None, MP_AXES),
            P(None, MP_AXES),
            P(MP_AXES, None),
            P(DP_AXES, None, MP_AXES, None, None),
            P(MP_AXES, None, None),
            P(None, None, None, MP_AXES, None),
            P(None, MP_AXES, None),
            P(MP_AXES, None, None),
            P(DP_AXES, None),
            P(DP_AXES, None),
            P(),
            P(),
        ),
        out_specs=(P(DP_AXES + MP_AXES, None), P(DP_AXES, None, MP_AXES, None)),
        check_vma=False,
    )
```

profile of v0, /device:TPU:1, one launch (start us, length us, event | category | flops | bytes accessed | tf_op | source)
XLA Modules:
  0.0 553.6 jit_solution(13675936725571163932)
XLA Ops:
  7.2 0.7 all-gather.4.cloned.1.call-update
  7.9 0.0 all-gather.6.cloned.1.call-start
  8.0 1.1 fusion.31
  9.0 1.0 fusion.33
  10.1 6.8 %all_gather.16 = bf16[32,4608]{1,0:T(8,128)(2,1)} all-gather(bf16[16,4608]{1,0:T(8,128)(2,1)S(1)} %fusion.33), channel_id=1, replica_groups=mesh['zh'=2,'c'=2,'x'=4,'y'=4,'zl'=2] {'zl'}, dimensions={0}, use_global_device_ids=true | all-gather | bytes 442368 | tf_op jit(solution)/shard_map/all_gather | solution.py:24
  16.8 0.0 reduce-scatter.5.cloned.1.call-start
  16.9 0.7 constant_dynamic-slice_fusion
  17.6 0.1 copy.46
  17.7 0.1 reshape.497
  17.8 0.7 fusion.72
  18.4 2.1 gather_fusion.2
  20.5 1.7 gather_fusion.1
  22.2 0.1 copy.47
  22.3 0.7 copy.48
  23.1 2.3 copy.60
  25.4 2.5 copy.50
  27.9 0.6 multiply_power_fusion
  28.5 0.6 add_select_fusion
  29.2 0.1 select_reduce_fusion.3
  29.2 0.1 select_reduce_fusion.1
  29.3 0.2 convert_reduce_fusion
  29.5 0.6 subtract_convert_fusion
  30.1 0.7 fusion.80
  30.8 0.6 iota_compare_fusion.2
  31.4 8.7 %all-gather.4.cloned.1.call-done = bf16[256,2,1,16,128]{4,3,2,1,0:T(8,128)(2,1)} async-done(((bf16[64,2,1,16,128]{4,3,2,1,0:T(8,128)(2,1)}), bf16[256,2,1,16,128]{4,3,2,1,0:T(8,128)(2,1)}) %all-gather.4.cloned.1.call-update) | async-done | bytes 2097168 | tf_op jit(solution)/shard_map/all_gather | solution.py:180
  40.0 2.9 gather_fusion
  42.9 1.7 fusion.81
  44.6 50.0 %all-gather.6.cloned.1.call-done = bf16[512,4608]{1,0:T(8,128)(2,1)} async-done(((bf16[32,4608]{1,0:T(8,128)(2,1)}), bf16[512,4608]{1,0:T(8,128)(2,1)}) %all-gather.6.cloned.1.call-update) | async-done | bytes 4718608 | tf_op jit(solution)/shard_map/all_gather | solution.py:24
  94.5 3.8 fusion.84
  98.4 6.8 %psum.28 = bf16[512,16]{0,1:T(8,128)(2,1)} all-reduce(bf16[512,16]{0,1:T(8,128)(2,1)S(1)} %select_reduce_fusion.2), channel_id=1, replica_groups=mesh['zh'=2,'c'=2,'x'=4,'y'=4,'zl'=2] {'zl'}, use_global_device_ids=true, to_apply=%region_4.5 | all-reduce | flops 8192 | bytes 32768 | tf_op jit(solution)/shard_map/psum | solution.py:36
  105.2 58.5 %psum.29 = bf16[512,16]{0,1:T(8,128)(2,1)S(1)} all-reduce(bf16[512,16]{0,1:T(8,128)(2,1)} %psum.28), channel_id=1, replica_groups=mesh['zh'=2,'c'=2,'x'=4,'y'=4,'zl'=2] {'x','y'}, use_global_device_ids=true, to_apply=%region_5.6 | all-reduce | flops 8192 | bytes 32768 | tf_op jit(solution)/shard_map/psum | solution.py:36
  163.7 0.7 broadcast_multiply_fusion
  164.4 1.3 convolution_bitcast_fusion
  165.8 3.9 fusion.19
  169.6 0.1 fusion.39
  169.8 1.7 fusion.22
  171.5 0.6 fusion.54
  172.2 0.5 fusion.82
  172.6 0.5 fusion.83
  173.2 0.3 fusion.26
  173.4 0.3 fusion.24
  173.7 0.2 fusion.86
  173.9 5.6 %psum.30 = f32[512,16]{0,1:T(8,128)S(1)} all-reduce(f32[512,16]{0,1:T(8,128)S(1)} %select_reduce_fusion), channel_id=1, replica_groups=mesh['zh'=2,'c'=2,'x'=4,'y'=4,'zl'=2] {'zl'}, use_global_device_ids=true, to_apply=%region_10.11 | all-reduce | flops 8192 | bytes 65536 | tf_op jit(solution)/shard_map/psum | solution.py:36
  179.5 55.6 %psum.31 = bf16[512,16]{0,1:T(8,128)(2,1)S(1)} all-reduce(f32[512,16]{0,1:T(8,128)S(1)} %psum.30), channel_id=1, replica_groups=mesh['zh'=2,'c'=2,'x'=4,'y'=4,'zl'=2] {'x','y'}, use_global_device_ids=true, to_apply=%region_11.12 | all-reduce | flops 8192 | bytes 49152 | tf_op jit(solution)/shard_map/psum | solution.py:36
  235.2 1.4 fusion.63
  236.6 3.5 fusion
  240.2 0.0 reduce-scatter.7.cloned.1.call-start
  240.2 105.5 %reduce-scatter.5.cloned.1.call-done = bf16[32,4608]{1,0:T(8,128)(2,1)} async-done(((bf16[512,4608]{1,0:T(8,128)(2,1)}), bf16[32,4608]{1,0:T(8,128)(2,1)}) %reduce-scatter.5.cloned.1.call-update) | async-done | bytes 294928 | tf_op jit(solution)/shard_map/reduce_scatter | solution.py:30
  345.7 0.0 all-gather.8.cloned.1.call-start
  345.8 17.8 %reduce-scatter.7.cloned.1.call-done = bf16[16,4608]{1,0:T(8,128)(2,1)} async-done(((bf16[32,4608]{1,0:T(8,128)(2,1)}), bf16[16,4608]{1,0:T(8,128)(2,1)}) %reduce-scatter.7.cloned.1.call-update) | async-done | bytes 147472 | tf_op jit(solution)/shard_map/reduce_scatter | solution.py:30
  363.6 1.1 fusion.27
  364.7 1.2 fusion.35
  365.8 0.1 fusion.37
  365.9 5.3 all_gather.18
  371.3 0.2 reduce-scatter.9.cloned.1.call-start
  371.5 55.4 %all-gather.8.cloned.1.call-done = bf16[512,4608]{1,0:T(8,128)(2,1)} async-done(((bf16[32,4608]{1,0:T(8,128)(2,1)}), bf16[512,4608]{1,0:T(8,128)(2,1)}) %all-gather.8.cloned.1.call-update) | async-done | bytes 4718608 | tf_op jit(solution)/shard_map/all_gather | solution.py:24
  427.0 7.4 %fusion.85 = f32[512,640]{1,0:T(8,128)S(1)} fusion(bf16[512,4608]{1,0:T(8,128)(2,1)} %all-gather.8.cloned.1.call-done, bf16[4608,640]{1,0:T(8,128)(2,1)} %param.28), kind=kOutput, calls=%fused_computation.141 | convolution fusion | flops 3019898880 | bytes 11927552 | tf_op jit(solution)/shard_map/dot_general | solution.py:217
  434.4 14.3 %convolution_convert_fusion = bf16[512,4608]{1,0:T(8,128)(2,1)} fusion(bf16[640,4608]{1,0:T(8,128)(2,1)} %param.30, bf16[512,4608]{1,0:T(8,128)(2,1)} %all-gather.8.cloned.1.call-done, bf16[4608,640]{1,0:T(8,128)(2,1)} %param.29, f32[512,640]{1,0:T(8,128)S(1)} %fusion.85), kind=kOutput, calls=%fused_computation.5 | convolution fusion | flops 6045433856 | bytes 22544384 | tf_op jit(solution)/shard_map/dot_general | solution.py:221
  448.7 0.0 reduce-scatter.11.cloned.1.call-start
  448.8 77.2 %reduce-scatter.9.cloned.1.call-done = bf16[32,4608]{1,0:T(8,128)(2,1)} async-done(((bf16[512,4608]{1,0:T(8,128)(2,1)}), bf16[32,4608]{1,0:T(8,128)(2,1)}) %reduce-scatter.9.cloned.1.call-update) | async-done | bytes 294928 | tf_op jit(solution)/shard_map/reduce_scatter | solution.py:30
  526.0 0.9 copy.52
  526.9 17.1 %reduce-scatter.11.cloned.1.call-done = bf16[16,4608]{1,0:T(8,128)(2,1)} async-done(((bf16[32,4608]{1,0:T(8,128)(2,1)}), bf16[16,4608]{1,0:T(8,128)(2,1)}) %reduce-scatter.11.cloned.1.call-update) | async-done | bytes 147472 | tf_op jit(solution)/shard_map/reduce_scatter | solution.py:30
  544.0 1.1 fusion.29
  545.1 1.7 fusion.38
  (69 shorter events, 0.4 us)
Async XLA Ops:
  7.2 229.4 %copy-start = (bf16[128,4608]{1,0:T(8,128)(2,1)S(1)}, bf16[128,4608]{1,0:T(8,128)(2,1)}, u32[]{:S(2)}) copy-start(bf16[128,4608]{1,0:T(8,128)(2,1)} %param.27) | copy-start | bytes 3538948
  7.2 32.9 %all-gather.4.cloned.1.call-start = ((), (), s32[]{:S(2)}) async-start(), calls=%async_computation.4 | async-start | bytes 2621440 | tf_op jit(solution)/shard_map/all_gather | solution.py:180
  7.9 86.6 %all-gather.6.cloned.1.call-start = ((), (), s32[]{:S(2)}) async-start(), calls=%async_computation.5 | async-start | bytes 5013504 | tf_op jit(solution)/shard_map/all_gather | solution.py:24
  16.8 328.9 %reduce-scatter.5.cloned.1.call-start = ((), (), s32[]{:S(2)}) async-start(), calls=%async_computation.6 | async-start | bytes 5013504 | tf_op jit(solution)/shard_map/reduce_scatter | solution.py:30
  23.1 6.1 %copy-start.9 = (s32[1,512]{1,0:T(1,128)S(1)}, s32[1,512]{1,0:T(1,128)}, u32[]{:S(2)}) copy-start(s32[1,512]{1,0:T(1,128)} %param.36) | copy-start | bytes 6148
  23.1 6.1 %copy-start.19 = (s32[1,8]{1,0:T(1,128)S(1)}, s32[1,8]{1,0:T(1,128)}, u32[]{:S(2)}) copy-start(s32[1,8]{1,0:T(1,128)} %param.37) | copy-start | bytes 100
  23.1 6.2 %copy-start.20 = (s32[64]{0:T(128)S(1)}, s32[64]{0:T(128)}, u32[]{:S(2)}) copy-start(s32[64]{0:T(128)} %param.38) | copy-start | bytes 772
  27.9 137.8 %copy-start.3 = (bf16[256,4608]{1,0:T(8,128)(2,1)S(1)}, bf16[256,4608]{1,0:T(8,128)(2,1)}, u32[]{:S(2)}) copy-start(bf16[256,4608]{1,0:T(8,128)(2,1)} %copy.50) | copy-start | bytes 7077892
  94.5 3.9 copy-start.17
  164.4 5.3 slice-start
  165.7 4.0 slice-start.1
  165.7 4.0 copy-start.5
  169.8 1.8 copy-start.16
  169.8 1.8 copy-start.21
  169.8 2.4 copy-start.8
  169.8 2.4 copy-start.10
  169.8 2.4 copy-start.18
  171.5 1.7 copy-start.7
  172.6 1.1 copy-start.2
  172.6 1.2 copy-start.14
  173.1 62.0 %copy-start.6 = (bf16[2,16,4608]{2,1,0:T(8,128)(2,1)S(1)}, bf16[2,16,4608]{2,1,0:T(8,128)(2,1)}, u32[]{:S(2)}) copy-start(bf16[2,16,4608]{2,1,0:T(8,128)(2,1)} %param.35) | copy-start | bytes 884740
  173.1 62.0 %copy-start.15 = (bf16[512,2]{0,1:T(2,128)(2,1)S(1)}, bf16[512,2]{0,1:T(2,128)(2,1)}, u32[]{:S(2)}) copy-start(bf16[512,2]{0,1:T(2,128)(2,1)} %get-tuple-element.14) | copy-start | bytes 6148
  240.1 124.5 %copy-start.4 = (bf16[16,4608]{1,0:T(8,128)(2,1)S(1)}, bf16[16,4608]{1,0:T(8,128)(2,1)}, u32[]{:S(2)}) copy-start(bf16[16,4608]{1,0:T(8,128)(2,1)} %param.20) | copy-start | bytes 442372
  240.1 124.5 %copy-start.11 = (f32[4608]{0:T(1024)S(1)}, f32[4608]{0:T(1024)}, u32[]{:S(2)}) copy-start(f32[4608]{0:T(1024)} %param.22) | copy-start | bytes 55300
  240.1 125.7 %copy-start.12 = (f32[4608]{0:T(1024)S(1)}, f32[4608]{0:T(1024)}, u32[]{:S(2)}) copy-start(f32[4608]{0:T(1024)} %param.23) | copy-start | bytes 55300
  240.2 123.4 %reduce-scatter.7.cloned.1.call-start = ((), (), s32[]{:S(2)}) async-start(), calls=%async_computation.7 | async-start | bytes 442368 | tf_op jit(solution)/shard_map/reduce_scatter | solution.py:30
  345.7 81.2 %all-gather.8.cloned.1.call-start = ((), (), s32[]{:S(2)}) async-start(), calls=%async_computation.8 | async-start | bytes 5013504 | tf_op jit(solution)/shard_map/all_gather | solution.py:24
  371.3 154.7 %reduce-scatter.9.cloned.1.call-start = ((), (), s32[]{:S(2)}) async-start(), calls=%async_computation.9 | async-start | bytes 5013504 | tf_op jit(solution)/shard_map/reduce_scatter | solution.py:30
  434.4 112.4 %copy-start.1 = (bf16[128,4608]{1,0:T(8,128)(2,1)S(1)}, bf16[128,4608]{1,0:T(8,128)(2,1)}, u32[]{:S(2)}) copy-start(bf16[128,4608]{1,0:T(8,128)(2,1)} %param.27) | copy-start | bytes 3538948
  448.7 96.3 %copy-start.13 = (f32[4608]{0:T(1024)S(1)}, f32[4608]{0:T(1024)}, u32[]{:S(2)}) copy-start(f32[4608]{0:T(1024)} %param.24) | copy-start | bytes 55300
  448.7 95.2 %reduce-scatter.11.cloned.1.call-start = ((), (), s32[]{:S(2)}) async-start(), calls=%async_computation.10 | async-start | bytes 442368 | tf_op jit(solution)/shard_map/reduce_scatter | solution.py:30
Sparse Core Ops, SparseCore 0:
  9.7 30.3 all-gather.3
  42.2 52.2 all-gather.5
  240.3 105.3 reduce-scatter.4
  347.9 15.6 reduce-scatter.6
  371.4 55.4 all-gather.7
  448.9 77.0 reduce-scatter.8
  528.3 15.6 reduce-scatter.10
where the time goes:
time: 554 us
  waiting for transfers between devices  332 us (60%)
  blocking collectives  139 us (25%)
  matrix products  39 us (7%)
  local copies, waits for them, and re-layouts  15.9 us (3%)
  between operations  14.6 us (3%)
  other arithmetic  12.7 us (2%)
    reduce_scatter x4, waiting for transfers between devices, scatter_mp(): values = lax.psum_scatter(values, stage, scatter_dimension=0, tiled=True)  218 us
    psum x4, blocking collectives, sum_mp(): values = lax.psum(values, stage)  127 us
    all_gather x2, waiting for transfers between devices, gather_mp(): values = lax.all_gather(values, stage, axis=0, tiled=True)  105 us
    dot_general x1, matrix products, shards(): jnp.dot(hidden, down_matrix, preferred_element_type=jnp.float32)  14.3 us
    all_gather x2, blocking collectives, gather_mp(): values = lax.all_gather(values, stage, axis=0, tiled=True)  12.1 us
  transfers between devices with their start and end apart: 7, of which 7 were waited for; matrix products, arithmetic and copies ran while one was open for 4% of the time, Pallas kernels for 0%

commit v1 on v0

--- a/solution.py
+++ b/solution.py
@@ -21,7 +21,10 @@
 
 def gather_mp(values):
     for stage in MP_STAGES:
-        values = lax.all_gather(values, stage, axis=0, tiled=True)
+        n_dev = lax.axis_size(stage)
+        blocks = jnp.stack([values for _ in range(n_dev)])
+        blocks = lax.all_to_all(blocks, stage, split_axis=0, concat_axis=0)
+        values = jnp.concatenate(blocks, axis=0)
     return values
 
 

time: 554 us -> 557 us (level)
  waiting for transfers between devices: 332 us -> 260 us
  blocking collectives: 139 us -> 207 us
  starting transfers between devices: 0.46 us -> 7.13 us
    all_gather x2 -> x0, waiting for transfers between devices: 105 us -> none  [gather_mp(): values = lax.all_gather(values, stage, axis=0, tiled=True)]
    all_to_all x0 -> x3, blocking collectives: none -> 76.2 us  [gather_mp(): blocks = lax.all_to_all(blocks, stage, split_axis=0, concat_axis=0)]
    all_to_all x0 -> x1, waiting for transfers between devices: none -> 19.8 us  [gather_mp(): blocks = lax.all_to_all(blocks, stage, split_axis=0, concat_axis=0)]
    all_gather x2 -> x0, blocking collectives: 12.1 us -> none  [gather_mp(): values = lax.all_gather(values, stage, axis=0, tiled=True)]
    all_gather x1, waiting for transfers between devices: 8.68 us -> 19.9 us  [shards(): whole_pool = lax.all_gather(key_value_cache, DP_AXES, axis=0, tiled=True)]
    all_to_all x0 -> x1, starting transfers between devices: none -> 6.93 us  [gather_mp(): blocks = lax.all_to_all(blocks, stage, split_axis=0, concat_axis=0)]
  transfers between devices with their start and end apart: 7 -> 6, of which waited for: 7 -> 6; matrix products, arithmetic and copies ran while one was open for 4% -> 3% of each run, Pallas kernels for 0% -> 0%
where the time goes in v1:
time: 557 us; the launch traced here: 556 us
  waiting for transfers between devices  260 us (47%)
  blocking collectives  207 us (37%)
  matrix products  36.6 us (7%)
  local copies, waits for them, and re-layouts  19.9 us (4%)
  between operations  14.2 us (3%)
  other arithmetic  11.5 us (2%)
  starting transfers between devices  7.13 us (1%)
    reduce_scatter x4, waiting for transfers between devices, scatter_mp(): values = lax.psum_scatter(values, stage, scatter_dimension=0, tiled=True)  220 us
    psum x4, blocking collectives, sum_mp(): values = lax.psum(values, stage)  130 us
    all_to_all x3, blocking collectives, gather_mp(): blocks = lax.all_to_all(blocks, stage, split_axis=0, concat_axis=0)  76.2 us
    all_gather x1, waiting for transfers between devices, shards(): whole_pool = lax.all_gather(key_value_cache, DP_AXES, axis=0, tiled=True)  19.9 us
    all_to_all x1, waiting for transfers between devices, gather_mp(): blocks = lax.all_to_all(blocks, stage, split_axis=0, concat_axis=0)  19.8 us
    dot_general x1, matrix products, shards(): jnp.dot(hidden, down_matrix, preferred_element_type=jnp.float32)  14.2 us
  transfers between devices with their start and end apart: 6, of which 6 were waited for; matrix products, arithmetic and copies ran while one was open for 3% of the time, Pallas kernels for 0%

profile of v1, /device:TPU:1, one launch (start us, length us, event | category | flops | bytes accessed | tf_op | source)
XLA Modules:
  0.0 556.2 jit_solution(9754967956445928960)
XLA Ops:
  7.2 1.2 fusion.26
  8.3 1.0 fusion.45
  9.4 8.2 %all_to_all.20 = bf16[2,16,4608]{2,1,0:T(8,128)(2,1)S(1)} all-to-all(bf16[2,16,4608]{2,1,0:T(8,128)(2,1)S(1)} %pad_maximum_fusion), channel_id=1, replica_groups=mesh['zh'=2,'c'=2,'x'=4,'y'=4,'zl'=2] {'zl'}, dimensions={0} | all-to-all | bytes 589824 | tf_op jit(solution)/shard_map/all_to_all | solution.py:26
  17.6 2.6 stack.27
  20.2 6.9 %all-to-all-start.1 = ((bf16[16,32,4608]{2,1,0:T(8,128)(2,1)}), bf16[16,32,4608]{2,1,0:T(8,128)(2,1)}, u32[]{:S(2)}, u32[]{:S(2)}) async-start(bf16[16,32,4608]{2,1,0:T(8,128)(2,1)} %stack.27), calls=%async_computation.1 | async-start | bytes 9437184 | tf_op jit(solution)/shard_map/all_to_all | solution.py:26
  27.2 0.0 all-gather.2.cloned.1.call-start
  27.2 0.7 all-gather.2.cloned.1.call-update
  27.9 0.7 constant_dynamic-slice_fusion
  28.6 0.1 copy.46
  28.7 0.1 reshape.507
  28.8 1.2 gather_fusion.2
  30.0 1.7 gather_fusion.1
  31.7 0.1 copy.47
  31.8 0.7 copy.48
  32.5 2.0 copy.60
  34.5 2.6 copy.50
  37.1 0.6 multiply_power_fusion
  37.7 0.6 add_select_fusion
  38.3 0.1 select_reduce_fusion.3
  38.4 0.1 select_reduce_fusion.1
  38.5 0.2 convert_reduce_fusion
  38.6 0.6 subtract_convert_fusion
  39.2 0.7 fusion.77
  39.9 0.6 iota_compare_fusion.2
  40.5 19.9 %all-gather.2.cloned.1.call-done = bf16[256,2,1,16,128]{4,3,2,1,0:T(8,128)(2,1)} async-done(((bf16[64,2,1,16,128]{4,3,2,1,0:T(8,128)(2,1)}), bf16[256,2,1,16,128]{4,3,2,1,0:T(8,128)(2,1)}) %all-gather.2.cloned.1.call-update) | async-done | bytes 2097168 | tf_op jit(solution)/shard_map/all_gather | solution.py:183
  60.3 2.9 gather_fusion
  63.2 1.7 fusion.78
  64.9 19.8 %all-to-all-done.1 = bf16[16,32,4608]{2,1,0:T(8,128)(2,1)} async-done(((bf16[16,32,4608]{2,1,0:T(8,128)(2,1)}), bf16[16,32,4608]{2,1,0:T(8,128)(2,1)}, u32[]{:S(2)}, u32[]{:S(2)}) %all-to-all-start.1) | async-done | bytes 4718624 | tf_op jit(solution)/shard_map/all_to_all | solution.py:26
  84.7 3.8 fusion.81
  88.5 8.0 %psum.28 = bf16[512,16]{0,1:T(8,128)(2,1)} all-reduce(bf16[512,16]{0,1:T(8,128)(2,1)S(1)} %select_reduce_fusion.2), channel_id=1, replica_groups=mesh['zh'=2,'c'=2,'x'=4,'y'=4,'zl'=2] {'zl'}, use_global_device_ids=true, to_apply=%region_4.5 | all-reduce | flops 8192 | bytes 32768 | tf_op jit(solution)/shard_map/psum | solution.py:39
  96.5 61.3 %psum.29 = bf16[512,16]{0,1:T(8,128)(2,1)S(1)} all-reduce(bf16[512,16]{0,1:T(8,128)(2,1)} %psum.28), channel_id=1, replica_groups=mesh['zh'=2,'c'=2,'x'=4,'y'=4,'zl'=2] {'x','y'}, use_global_device_ids=true, to_apply=%region_5.6 | all-reduce | flops 8192 | bytes 32768 | tf_op jit(solution)/shard_map/psum | solution.py:39
  157.8 3.8 convolution_bitcast_fusion.1
  161.7 0.2 convolution_bitcast_fusion
  162.0 4.1 fusion.17
  166.1 0.1 fusion.34
  166.2 0.6 fusion.51
  166.9 0.5 fusion.79
  167.4 0.5 fusion.80
  167.9 0.2 fusion.21
  168.1 0.3 fusion.19
  168.4 0.2 fusion.83
  168.6 5.5 psum.30
  174.1 55.6 %psum.31 = bf16[512,16]{0,1:T(8,128)(2,1)S(1)} all-reduce(f32[512,16]{0,1:T(8,128)S(1)} %psum.30), channel_id=1, replica_groups=mesh['zh'=2,'c'=2,'x'=4,'y'=4,'zl'=2] {'x','y'}, use_global_device_ids=true, to_apply=%region_11.12 | all-reduce | flops 8192 | bytes 49152 | tf_op jit(solution)/shard_map/psum | solution.py:39
  229.7 1.4 fusion.60
  231.2 3.5 fusion
  234.7 0.0 reduce-scatter.7.cloned.1.call-start
  234.8 107.7 %reduce-scatter.5.cloned.1.call-done = bf16[32,4608]{1,0:T(8,128)(2,1)} async-done(((bf16[512,4608]{1,0:T(8,128)(2,1)}), bf16[32,4608]{1,0:T(8,128)(2,1)}) %reduce-scatter.5.cloned.1.call-update) | async-done | bytes 294928 | tf_op jit(solution)/shard_map/reduce_scatter | solution.py:33
  342.5 0.0 reduce-scatter.9.cloned.1.call-start
  342.5 17.9 %reduce-scatter.7.cloned.1.call-done = bf16[16,4608]{1,0:T(8,128)(2,1)} async-done(((bf16[32,4608]{1,0:T(8,128)(2,1)}), bf16[16,4608]{1,0:T(8,128)(2,1)}) %reduce-scatter.7.cloned.1.call-update) | async-done | bytes 147472 | tf_op jit(solution)/shard_map/reduce_scatter | solution.py:33
  360.4 1.1 fusion.22
  361.5 1.2 fusion.30
  362.7 0.1 fusion.44
  362.8 7.1 %all_to_all.21 = bf16[2,16,4608]{2,1,0:T(8,128)(2,1)S(1)} all-to-all(bf16[2,16,4608]{2,1,0:T(8,128)(2,1)S(1)} %pad_maximum_fusion.1), channel_id=1, replica_groups=mesh['zh'=2,'c'=2,'x'=4,'y'=4,'zl'=2] {'zl'}, dimensions={0} | all-to-all | bytes 589824 | tf_op jit(solution)/shard_map/all_to_all | solution.py:26
  370.0 0.4 stack.30
  370.5 60.9 %all_to_all.22 = bf16[16,32,4608]{2,1,0:T(8,128)(2,1)S(1)} all-to-all(bf16[16,32,4608]{2,1,0:T(8,128)(2,1)S(1)} %stack.30), channel_id=1, replica_groups=mesh['zh'=2,'c'=2,'x'=4,'y'=4,'zl'=2] {'x','y'}, dimensions={0} | all-to-all | bytes 9437184 | tf_op jit(solution)/shard_map/all_to_all | solution.py:26
  431.4 2.2 copy-done.2
  433.5 3.8 fusion.82
  437.4 14.2 %convolution_convert_fusion = bf16[512,4608]{1,0:T(8,128)(2,1)} fusion(bf16[640,4608]{1,0:T(8,128)(2,1)} %param.30, bf16[512,4608]{1,0:T(8,128)(2,1)} %bitcast.108, bf16[4608,640]{1,0:T(8,128)(2,1)} %param.29, f32[512,640]{1,0:T(8,128)S(1)} %fusion.82), kind=kOutput, calls=%fused_computation.5 | convolution fusion | flops 6045433856 | bytes 22544384 | tf_op jit(solution)/shard_map/dot_general | solution.py:224
  451.6 0.0 reduce-scatter.11.cloned.1.call-start
  451.7 77.5 %reduce-scatter.9.cloned.1.call-done = bf16[32,4608]{1,0:T(8,128)(2,1)} async-done(((bf16[512,4608]{1,0:T(8,128)(2,1)}), bf16[32,4608]{1,0:T(8,128)(2,1)}) %reduce-scatter.9.cloned.1.call-update) | async-done | bytes 294928 | tf_op jit(solution)/shard_map/reduce_scatter | solution.py:33
  529.2 0.9 copy.52
  530.1 16.9 %reduce-scatter.11.cloned.1.call-done = bf16[16,4608]{1,0:T(8,128)(2,1)} async-done(((bf16[32,4608]{1,0:T(8,128)(2,1)}), bf16[16,4608]{1,0:T(8,128)(2,1)}) %reduce-scatter.11.cloned.1.call-update) | async-done | bytes 147472 | tf_op jit(solution)/shard_map/reduce_scatter | solution.py:33
  546.9 1.1 fusion.24
  548.0 1.7 fusion.33
  (78 shorter events, 0.5 us)
Async XLA Ops:
  7.2 224.0 %copy-start = (bf16[128,4608]{1,0:T(8,128)(2,1)S(1)}, bf16[128,4608]{1,0:T(8,128)(2,1)}, u32[]{:S(2)}) copy-start(bf16[128,4608]{1,0:T(8,128)(2,1)} %param.27) | copy-start | bytes 3538948
  20.2 8.6 %copy-start.23 = (s32[1,8]{1,0:T(1,128)S(1)}, s32[1,8]{1,0:T(1,128)}, u32[]{:S(2)}) copy-start(s32[1,8]{1,0:T(1,128)} %param.37) | copy-start | bytes 100
  20.2 8.6 %copy-start.9 = (bf16[64,128,16]{1,2,0:T(8,128)(2,1)S(1)}, bf16[64,128,16]{1,2,0:T(8,128)(2,1)}, u32[]{:S(2)}) copy-start(bf16[64,128,16]{1,2,0:T(8,128)(2,1)} %param.34) | copy-start | bytes 786436
  20.2 64.4 %all-to-all-start.1 = ((bf16[16,32,4608]{2,1,0:T(8,128)(2,1)}), bf16[16,32,4608]{2,1,0:T(8,128)(2,1)}, u32[]{:S(2)}, u32[]{:S(2)}) async-start(bf16[16,32,4608]{2,1,0:T(8,128)(2,1)} %stack.27), calls=%async_computation.1 | async-start | bytes 9437184 | tf_op jit(solution)/shard_map/all_to_all | solution.py:26
  27.2 33.2 %all-gather.2.cloned.1.call-start = ((), (), s32[]{:S(2)}) async-start(), calls=%async_computation.8 | async-start | bytes 2621440 | tf_op jit(solution)/shard_map/all_gather | solution.py:183
  27.9 314.6 %reduce-scatter.5.cloned.1.call-start = ((), (), s32[]{:S(2)}) async-start(), calls=%async_computation.9 | async-start | bytes 5013504 | tf_op jit(solution)/shard_map/reduce_scatter | solution.py:33
  32.5 5.7 %copy-start.13 = (s32[1,512]{1,0:T(1,128)S(1)}, s32[1,512]{1,0:T(1,128)}, u32[]{:S(2)}) copy-start(s32[1,512]{1,0:T(1,128)} %param.36) | copy-start | bytes 6148
  32.5 5.8 %copy-start.24 = (s32[64]{0:T(128)S(1)}, s32[64]{0:T(128)}, u32[]{:S(2)}) copy-start(s32[64]{0:T(128)} %param.38) | copy-start | bytes 772
  37.1 120.7 %copy-start.4 = (bf16[256,4608]{1,0:T(8,128)(2,1)S(1)}, bf16[256,4608]{1,0:T(8,128)(2,1)}, u32[]{:S(2)}) copy-start(bf16[256,4608]{1,0:T(8,128)(2,1)} %copy.50) | copy-start | bytes 7077892
  84.7 3.9 copy-start.21
  157.8 3.9 copy-start.12
  157.8 3.9 copy-start.7
  157.8 4.2 copy-start.6
  162.0 4.2 copy-start.20
  162.0 4.2 copy-start.25
  162.0 4.8 copy-start.11
  162.0 4.8 copy-start.14
  162.0 4.8 copy-start.22
  166.1 1.7 copy-start.10
  167.3 1.1 copy-start.3
  167.4 1.2 copy-start.18
  167.8 61.9 %copy-start.8 = (bf16[2,16,4608]{2,1,0:T(8,128)(2,1)S(1)}, bf16[2,16,4608]{2,1,0:T(8,128)(2,1)}, u32[]{:S(2)}) copy-start(bf16[2,16,4608]{2,1,0:T(8,128)(2,1)} %param.35) | copy-start | bytes 884740
  167.8 61.9 %copy-start.19 = (bf16[512,2]{0,1:T(2,128)(2,1)S(1)}, bf16[512,2]{0,1:T(2,128)(2,1)}, u32[]{:S(2)}) copy-start(bf16[512,2]{0,1:T(2,128)(2,1)} %get-tuple-element.14) | copy-start | bytes 6148
  234.7 126.8 %copy-start.5 = (bf16[16,4608]{1,0:T(8,128)(2,1)S(1)}, bf16[16,4608]{1,0:T(8,128)(2,1)}, u32[]{:S(2)}) copy-start(bf16[16,4608]{1,0:T(8,128)(2,1)} %param.20) | copy-start | bytes 442372
  234.7 126.8 %copy-start.15 = (f32[4608]{0:T(1024)S(1)}, f32[4608]{0:T(1024)}, u32[]{:S(2)}) copy-start(f32[4608]{0:T(1024)} %param.22) | copy-start | bytes 55300
  234.7 128.0 %copy-start.16 = (f32[4608]{0:T(1024)S(1)}, f32[4608]{0:T(1024)}, u32[]{:S(2)}) copy-start(f32[4608]{0:T(1024)} %param.23) | copy-start | bytes 55300
  234.7 125.7 %reduce-scatter.7.cloned.1.call-start = ((), (), s32[]{:S(2)}) async-start(), calls=%async_computation.10 | async-start | bytes 442368 | tf_op jit(solution)/shard_map/reduce_scatter | solution.py:33
  342.5 186.7 %reduce-scatter.9.cloned.1.call-start = ((), (), s32[]{:S(2)}) async-start(), calls=%async_computation.11 | async-start | bytes 5013504 | tf_op jit(solution)/shard_map/reduce_scatter | solution.py:33
  370.0 63.5 %slice-start = ((s8[5898240]{0:T(1024)(128)(4,1)}), s8[4194304]{0:T(1024)(128)(4,1)S(1)}, s32[]{:S(2)}) async-start(s8[5898240]{0:T(1024)(128)(4,1)} %bitcast.136), calls=%async_computation.13 | async-start | bytes 8388608
  370.4 63.1 %slice-start.1 = ((s8[5898240]{0:T(1024)(128)(4,1)}), s8[1703936]{0:T(1024)(128)(4,1)S(1)}, s32[]{:S(2)}) async-start(s8[5898240]{0:T(1024)(128)(4,1)} %bitcast.136), calls=%async_computation.14 | async-start | bytes 3407872
  431.4 2.2 copy-start.2
  437.3 112.4 %copy-start.1 = (bf16[128,4608]{1,0:T(8,128)(2,1)S(1)}, bf16[128,4608]{1,0:T(8,128)(2,1)}, u32[]{:S(2)}) copy-start(bf16[128,4608]{1,0:T(8,128)(2,1)} %param.27) | copy-start | bytes 3538948
  451.6 96.4 %copy-start.17 = (f32[4608]{0:T(1024)S(1)}, f32[4608]{0:T(1024)}, u32[]{:S(2)}) copy-start(f32[4608]{0:T(1024)} %param.24) | copy-start | bytes 55300
  451.6 95.3 %reduce-scatter.11.cloned.1.call-start = ((), (), s32[]{:S(2)}) async-start(), calls=%async_computation.12 | async-start | bytes 442368 | tf_op jit(solution)/shard_map/reduce_scatter | solution.py:33
Sparse Core Ops, SparseCore 0:
  29.6 30.6 all-gather.1
  234.9 107.5 reduce-scatter.4
  344.8 15.5 reduce-scatter.6
  451.7 77.3 reduce-scatter.8
  531.3 15.5 reduce-scatter.10
